TPU v7x, 512 devices: a whole 4x8x8 slice. The times are simulated.
512 devices in a mesh: dp: 8 (over z), expert: 16 (over y, core), etp: 4 (over x).
Axes of the slice: x: 4, y: 8, z: 8, core: 2. Of those that a mesh axis runs over, the one named last changes fastest.
Arguments:
- tokens: bfloat16 [3072, 4096], P(('dp', 'expert')), may hold values from -6 to 6
- cotangent: bfloat16 [3072, 4096], P(('dp', 'expert')), may hold values from -3 to 3
- route_weights: float32 [3072, 8], P(('dp', 'expert')), may hold values from 0.05 to 0.3
- expert_ids: int32 [3072, 8], P(('dp', 'expert')), may hold values from 0 to 15, as said below
- w_gate: bfloat16 [16, 1536, 4096], P('expert', 'etp', 'dp'), may hold values from -0.09375 to 0.09375
- w_up: bfloat16 [16, 1536, 4096], P('expert', 'etp', 'dp'), may hold values from -0.09375 to 0.09375
- w_down: bfloat16 [16, 1536, 4096], P('expert', 'etp', 'dp'), may hold values from -0.15625 to 0.15625
Outputs:
- mixed: bfloat16 [3072, 4096], P(('dp', 'expert'), 'etp')
- grad_tokens: bfloat16 [3072, 4096], P(('dp', 'expert'), 'etp')
- grad_gate: float32 [16, 1536, 4096], P('expert', 'etp', 'dp')
Inputs may be any that keep to these rules, and one draw needn't show every extreme that they name: `expert_ids`: each row names 8 different experts. Within each aligned block of 24 rows no expert is named by more than 16 rows; in every run of 16 consecutive blocks starting at a multiple of 16, one expert is named by exactly 16 rows of every block.
All inputs are finite; a program needn't handle non-finite values.
Results may differ from a plain program's by a relative error of at most 0.012.
Values may be sent and summed in bfloat16 or wider, within the bound.
No kernel may reach another device: no remote copies, remote signals or barrier semaphores. Data moves between devices by JAX's collectives and lax.ppermute only.
A program may use at most 64 MiB of HBM per device.

v0:
```python
import jax
import jax.numpy as jnp
from jax import lax
from jax.sharding import PartitionSpec as P


def on_device(tokens, cotangent, route_weights, expert_ids, w_gate, w_up, w_down):
    tok_count, model_width = tokens.shape
    top_count = expert_ids.shape[1]
    experts = lax.axis_size("expert")
    capacity = tok_count // experts * top_count + min(top_count, tok_count % experts)
    slot_rows = experts * capacity
    named_count = jnp.sum(
        (expert_ids[:, :, None] == jnp.arange(experts, dtype=jnp.int32)).astype(jnp.int32), axis=1
    )
    before = jnp.cumsum(named_count, axis=0) - named_count
    position = jnp.take_along_axis(before, expert_ids, axis=1)
    slot_index = (expert_ids * capacity + position).reshape(-1)
    copies = jnp.broadcast_to(tokens[:, None, :], (tok_count, top_count, model_width)).reshape(
        -1, model_width
    )
    scaled = (
        (route_weights[:, :, None] * cotangent[:, None, :].astype(jnp.float32))
        .astype(jnp.bfloat16)
        .reshape(-1, model_width)
    )
    empty_slots = jnp.zeros((slot_rows, model_width), jnp.bfloat16)
    send_rows = empty_slots.at[slot_index].set(copies).reshape(experts, capacity, model_width)
    send_grads = empty_slots.at[slot_index].set(scaled).reshape(experts, capacity, model_width)
    recv_rows, recv_grads = (
        lax.all_to_all(send_rows, "expert", split_axis=0, concat_axis=0, tiled=True),
        lax.all_to_all(send_grads, "expert", split_axis=0, concat_axis=0, tiled=True),
    )
    flat_rows = recv_rows.reshape(slot_rows, model_width)
    flat_grads = recv_grads.reshape(slot_rows, model_width)
    gate_full, up_full, down_full = (
        lax.all_gather(w_gate[0], "dp", axis=1, tiled=True),
        lax.all_gather(w_up[0], "dp", axis=1, tiled=True),
        lax.all_gather(w_down[0], "dp", axis=1, tiled=True),
    )
    contract_last = (((1,), (1,)), ((), ()))
    gate_value = lax.dot_general(
        flat_rows, gate_full, contract_last, preferred_element_type=jnp.float32
    )
    up_value = lax.dot_general(
        flat_rows, up_full, contract_last, preferred_element_type=jnp.float32
    )
    sigmoid_gate = jax.nn.sigmoid(gate_value)
    active = gate_value * sigmoid_gate
    hidden = (active * up_value).astype(jnp.bfloat16)
    mixed_slots = jnp.dot(hidden, down_full, preferred_element_type=jnp.float32).astype(
        jnp.bfloat16
    )
    d_hidden = lax.dot_general(
        flat_grads, down_full, contract_last, preferred_element_type=jnp.float32
    )
    d_gate = (
        d_hidden * up_value * sigmoid_gate * (1.0 + gate_value * (1.0 - sigmoid_gate))
    ).astype(jnp.bfloat16)
    d_up = (d_hidden * active).astype(jnp.bfloat16)
    input_slots = (
        jnp.dot(d_gate, gate_full, preferred_element_type=jnp.float32)
        + jnp.dot(d_up, up_full, preferred_element_type=jnp.float32)
    ).astype(jnp.bfloat16)
    weight_grads = lax.psum_scatter(
        lax.dot_general(
            flat_rows, d_gate, (((0,), (0,)), ((), ())), preferred_element_type=jnp.float32
        ).astype(jnp.bfloat16),
        "dp",
        scatter_dimension=0,
        tiled=True,
    ).astype(jnp.float32)
    grad_gate = jnp.transpose(weight_grads)[None]
    back_mixed, back_input = (
        lax.all_to_all(
            mixed_slots.reshape(experts, capacity, model_width),
            "expert",
            split_axis=0,
            concat_axis=0,
            tiled=True,
        ),
        lax.all_to_all(
            input_slots.reshape(experts, capacity, model_width),
            "expert",
            split_axis=0,
            concat_axis=0,
            tiled=True,
        ),
    )
    token_mixed = back_mixed.reshape(slot_rows, model_width)[slot_index].reshape(
        tok_count, top_count, model_width
    )
    token_input = back_input.reshape(slot_rows, model_width)[slot_index].reshape(
        tok_count, top_count, model_width
    )
    mixed_part = jnp.sum(route_weights[:, :, None] * token_mixed.astype(jnp.float32), axis=1)
    input_part = jnp.sum(token_input.astype(jnp.float32), axis=1)
    mixed, grad_tokens = (
        lax.psum_scatter(
            mixed_part.astype(jnp.bfloat16), "etp", scatter_dimension=1, tiled=True
        ).astype(jnp.float32),
        lax.psum_scatter(
            input_part.astype(jnp.bfloat16), "etp", scatter_dimension=1, tiled=True
        ).astype(jnp.float32),
    )
    return (mixed.astype(jnp.bfloat16), grad_tokens.astype(jnp.bfloat16), grad_gate)


def solution(mesh):
    in_specs = (
        P(("dp", "expert"), None),
        P(("dp", "expert"), None),
        P(("dp", "expert"), None),
        P(("dp", "expert"), None),
        P("expert", "etp", "dp"),
        P("expert", "etp", "dp"),
        P("expert", "etp", "dp"),
    )
    out_specs = (P(("dp", "expert"), "etp"), P(("dp", "expert"), "etp"), P("expert", "etp", "dp"))
    return jax.shard_map(
        on_device, mesh=mesh, in_specs=in_specs, out_specs=out_specs, check_vma=False
    )
```

profile of v0, /device:TPU:8, one launch (start us, length us, event | category | flops | bytes accessed | tf_op | source)
XLA Modules:
  0.0 312.0 jit_solution(12427213311101825373)
XLA Ops:
  10.4 1.6 gather_fusion.2
  12.2 4.4 %scatter_custom_fusion = bf16[256,4096]{1,0:T(8,128)(2,1)} fusion(s32[192]{0:T(256)S(1)} %bitcast.61, bf16[]{:T(256)} %constant.10.clone.1, bf16[24,4096]{1,0:T(8,128)(2,1)S(1)} %copy-done), kind=kCustom, calls=%fused_computation.25 | custom fusion | bytes 2293762 | tf_op jit(solution)/shard_map/scatter | solution.py:28
  16.6 9.5 %all-to-all-start = ((bf16[16,16,4096]{2,1,0:T(8,128)(2,1)}), bf16[16,16,4096]{2,1,0:T(8,128)(2,1)S(1)}, u32[]{:S(2)}, u32[]{:S(2)}) async-start(bf16[16,16,4096]{2,1,0:T(8,128)(2,1)} %bitcast.59), calls=%async_computation | async-start | bytes 4194304 | tf_op jit(solution)/shard_map/all_to_all | solution.py:31
  27.0 4.3 %scatter_custom_fusion.1 = bf16[256,4096]{1,0:T(8,128)(2,1)} fusion(s32[192]{0:T(256)S(1)} %bitcast.62, f32[24,4096]{1,0:T(8,128)S(1)} %convert_element_type.51, f32[192]{0:T(256)S(1)} %mul.59, bf16[]{:T(256)} %constant.10.clone.1), kind=kCustom, calls=%fused_computation.23 | custom fusion | flops 1572864 | bytes 2491394 | tf_op jit(solution)/shard_map/scatter | solution.py:29
  31.3 42.1 %all-to-all-done = bf16[16,16,4096]{2,1,0:T(8,128)(2,1)S(1)} async-done(((bf16[16,16,4096]{2,1,0:T(8,128)(2,1)}), bf16[16,16,4096]{2,1,0:T(8,128)(2,1)S(1)}, u32[]{:S(2)}, u32[]{:S(2)}) %all-to-all-start) | async-done | bytes 2097184 | tf_op jit(solution)/shard_map/all_to_all | solution.py:31
  73.4 6.6 %all-to-all-start.2 = ((bf16[16,16,4096]{2,1,0:T(8,128)(2,1)}), bf16[16,16,4096]{2,1,0:T(8,128)(2,1)}, u32[]{:S(2)}, u32[]{:S(2)}) async-start(bf16[16,16,4096]{2,1,0:T(8,128)(2,1)} %bitcast.60), calls=%async_computation.3 | async-start | bytes 4194304 | tf_op jit(solution)/shard_map/all_to_all | solution.py:32
  80.0 3.9 %fusion.7 = f32[256,384]{1,0:T(8,128)} fusion(bf16[256,4096]{1,0:T(8,128)(2,1)S(1)} %bitcast.54, bf16[1,384,4096]{2,1,0:T(8,128)(2,1)} %all-gather.9.cloned.1.call-done), kind=kOutput, calls=%fused_computation.17 | convolution fusion | flops 805306368 | bytes 5636096 | tf_op jit(solution)/shard_map/dot_general | solution.py:45
  83.9 43.6 %all-to-all-done.2 = bf16[16,16,4096]{2,1,0:T(8,128)(2,1)} async-done(((bf16[16,16,4096]{2,1,0:T(8,128)(2,1)}), bf16[16,16,4096]{2,1,0:T(8,128)(2,1)}, u32[]{:S(2)}, u32[]{:S(2)}) %all-to-all-start.2) | async-done | bytes 2097184 | tf_op jit(solution)/shard_map/all_to_all | solution.py:32
  127.5 3.8 %fusion.3 = f32[256,384]{1,0:T(8,128)S(1)} fusion(bf16[256,4096]{1,0:T(8,128)(2,1)} %bitcast.13, bf16[1,384,4096]{2,1,0:T(8,128)(2,1)} %all-gather.11.cloned.1.call-done), kind=kOutput, calls=%fused_computation.13 | convolution fusion | flops 805306368 | bytes 5636096 | tf_op jit(solution)/shard_map/dot_general | solution.py:54
  131.3 29.1 %all-gather.7.cloned.1.call-done = bf16[1,384,4096]{2,1,0:T(8,128)(2,1)} async-done(((bf16[1,384,512]{2,1,0:T(8,128)(2,1)}), bf16[1,384,4096]{2,1,0:T(8,128)(2,1)}) %all-gather.7.cloned.1.call-update) | async-done | bytes 3145744 | tf_op jit(solution)/shard_map/all_gather | solution.py:37
  160.4 3.4 %multiply_convert_fusion.1 = (bf16[256,384]{1,0:T(8,128)(2,1)S(1)}, f32[256,384]{1,0:T(8,128)S(1)}) fusion(f32[256,384]{1,0:T(8,128)S(1)} %fusion.3, f32[256,384]{1,0:T(8,128)} %fusion.7, bf16[256,4096]{1,0:T(8,128)(2,1)S(1)} %bitcast.55, bf16[1,384,4096]{2,1,0:T(8,128)(2,1)} %all-gather.7.cloned.1.call-done), kind=kOutput, calls=%fused_computation.34 | convolution fusion | flops 806289408 | bytes 6619136 | tf_op jit(solution)/shard_map/dot_general | solution.py:42
  163.8 2.6 convolution_convert_fusion.1
  166.4 7.3 %all-to-all-start.1 = ((bf16[16,16,4096]{2,1,0:T(8,128)(2,1)}), bf16[16,16,4096]{2,1,0:T(8,128)(2,1)S(1)}, u32[]{:S(2)}, u32[]{:S(2)}) async-start(bf16[16,16,4096]{2,1,0:T(8,128)(2,1)} %bitcast.58), calls=%async_computation.1 | async-start | bytes 4194304 | tf_op jit(solution)/shard_map/all_to_all | solution.py:75
  173.8 4.6 %convolution_convert_fusion = bf16[4096,384]{1,0:T(8,128)(2,1)} fusion(bf16[256,4096]{1,0:T(8,128)(2,1)} %bitcast.56, bf16[256,384]{1,0:T(8,128)(2,1)S(1)} %get-tuple-element.12), kind=kOutput, calls=%fused_computation.5 | convolution fusion | flops 806879232 | bytes 5439488 | tf_op jit(solution)/shard_map/dot_general | solution.py:66
  178.4 3.3 %fusion.9 = f32[256,4096]{1,0:T(8,128)S(1)} fusion(bf16[256,384]{1,0:T(8,128)(2,1)S(1)} %get-tuple-element.12, bf16[1,384,4096]{2,1,0:T(8,128)(2,1)} %all-gather.7.cloned.1.call-done), kind=kOutput, calls=%fused_computation.19 | convolution fusion | flops 805306368 | bytes 7536640 | tf_op jit(solution)/shard_map/dot_general | solution.py:62
  181.7 2.7 fusion
  184.3 36.8 %all-to-all-done.1 = bf16[16,16,4096]{2,1,0:T(8,128)(2,1)S(1)} async-done(((bf16[16,16,4096]{2,1,0:T(8,128)(2,1)}), bf16[16,16,4096]{2,1,0:T(8,128)(2,1)S(1)}, u32[]{:S(2)}, u32[]{:S(2)}) %all-to-all-start.1) | async-done | bytes 2097184 | tf_op jit(solution)/shard_map/all_to_all | solution.py:75
  221.1 6.5 %all-to-all-start.3 = ((bf16[16,16,4096]{2,1,0:T(8,128)(2,1)}), bf16[16,16,4096]{2,1,0:T(8,128)(2,1)}, u32[]{:S(2)}, u32[]{:S(2)}) async-start(bf16[16,16,4096]{2,1,0:T(8,128)(2,1)} %bitcast.57), calls=%async_computation.4 | async-start | bytes 4194304 | tf_op jit(solution)/shard_map/all_to_all | solution.py:82
  227.7 2.7 gather_fusion
  230.4 3.3 %fusion.1 = bf16[24,4096]{1,0:T(8,128)(2,1)} fusion(bf16[192,4096]{1,0:T(8,128)(2,1)} %gather_fusion, f32[24,8]{1,0:T(8,128)S(1)} %copy.21), kind=kLoop, calls=%fused_computation.10 | loop fusion | flops 2260992 | bytes 1770240 | tf_op jit(solution)/shard_map/reduce_sum | solution.py:96
  233.8 41.3 %all-to-all-done.3 = bf16[16,16,4096]{2,1,0:T(8,128)(2,1)} async-done(((bf16[16,16,4096]{2,1,0:T(8,128)(2,1)}), bf16[16,16,4096]{2,1,0:T(8,128)(2,1)}, u32[]{:S(2)}, u32[]{:S(2)}) %all-to-all-start.3) | async-done | bytes 2097184 | tf_op jit(solution)/shard_map/all_to_all | solution.py:82
  275.1 4.9 %gather_fusion.1 = bf16[192,4096]{1,0:T(8,128)(2,1)S(1)} fusion(bf16[256,4096]{1,0:T(8,128)(2,1)} %bitcast.15, s32[1024]{0:T(1024)S(1)} %pad_clamp_fusion), kind=kCustom, calls=%fused_computation.1 | custom fusion | bytes 3146496 | tf_op jit(solution)/shard_map/gather | solution.py:93
  280.1 1.7 bitcast_reduce_fusion
  284.0 21.1 %reduce-scatter.6.cloned.1.call-done = bf16[24,1024]{1,0:T(8,128)(2,1)} async-done(((bf16[24,4096]{1,0:T(8,128)(2,1)}), bf16[24,1024]{1,0:T(8,128)(2,1)}) %reduce-scatter.6.cloned.1.call-update) | async-done | bytes 49168 | tf_op jit(solution)/shard_map/reduce_scatter | solution.py:102
  (47 shorter events, 6.7 us)
Async XLA Ops:
  7.2 5.0 %copy-start = (bf16[24,4096]{1,0:T(8,128)(2,1)S(1)}, bf16[24,4096]{1,0:T(8,128)(2,1)}, u32[]{:S(2)}) copy-start(bf16[24,4096]{1,0:T(8,128)(2,1)} %param.7) | copy-start | bytes 589828
  7.2 72.8 %all-gather.9.cloned.1.call-start = ((), (), s32[]{:S(2)}) async-start(), calls=%async_computation.11 | async-start | bytes 3538944 | tf_op jit(solution)/shard_map/all_gather | solution.py:38
  7.9 119.6 %all-gather.11.cloned.1.call-start = ((), (), s32[]{:S(2)}) async-start(), calls=%async_computation.12 | async-start | bytes 3538944 | tf_op jit(solution)/shard_map/all_gather | solution.py:39
  16.6 10.2 %copy-start.5 = (bf16[24,4096]{1,0:T(8,128)(2,1)S(1)}, bf16[24,4096]{1,0:T(8,128)(2,1)}, u32[]{:S(2)}) copy-start(bf16[24,4096]{1,0:T(8,128)(2,1)} %param.8) | copy-start | bytes 589828
  16.6 10.3 %copy-start.6 = (f32[24,8]{0,1:T(8,128)S(1)}, f32[24,8]{0,1:T(8,128)}, u32[]{:S(2)}) copy-start(f32[24,8]{0,1:T(8,128)} %param.9) | copy-start | bytes 2308
  16.6 56.9 %all-to-all-start = ((bf16[16,16,4096]{2,1,0:T(8,128)(2,1)}), bf16[16,16,4096]{2,1,0:T(8,128)(2,1)S(1)}, u32[]{:S(2)}, u32[]{:S(2)}) async-start(bf16[16,16,4096]{2,1,0:T(8,128)(2,1)} %bitcast.59), calls=%async_computation | async-start | bytes 4194304 | tf_op jit(solution)/shard_map/all_to_all | solution.py:31
  26.0 134.3 %all-gather.7.cloned.1.call-start = ((), (), s32[]{:S(2)}) async-start(), calls=%async_computation.10 | async-start | bytes 3538944 | tf_op jit(solution)/shard_map/all_gather | solution.py:37
  73.4 86.9 %copy-start.1 = (bf16[16,16,4096]{2,1,0:T(8,128)(2,1)}, bf16[16,16,4096]{2,1,0:T(8,128)(2,1)S(1)}, u32[]{:S(2)}) copy-start(bf16[16,16,4096]{2,1,0:T(8,128)(2,1)S(1)} %all-to-all-done) | copy-start | bytes 6291460
  73.4 54.1 %all-to-all-start.2 = ((bf16[16,16,4096]{2,1,0:T(8,128)(2,1)}), bf16[16,16,4096]{2,1,0:T(8,128)(2,1)}, u32[]{:S(2)}, u32[]{:S(2)}) async-start(bf16[16,16,4096]{2,1,0:T(8,128)(2,1)} %bitcast.60), calls=%async_computation.3 | async-start | bytes 4194304 | tf_op jit(solution)/shard_map/all_to_all | solution.py:32
  160.4 3.4 %copy-start.2 = (bf16[1,384,4096]{2,1,0:T(8,128)(2,1)S(1)}, bf16[1,384,4096]{2,1,0:T(8,128)(2,1)}, u32[]{:S(2)}) copy-start(bf16[1,384,4096]{2,1,0:T(8,128)(2,1)} %all-gather.11.cloned.1.call-done) | copy-start | bytes 9437188
  160.4 3.5 %copy-start.4 = (f32[256,384]{1,0:T(8,128)S(1)}, f32[256,384]{1,0:T(8,128)}, u32[]{:S(2)}) copy-start(f32[256,384]{1,0:T(8,128)} %fusion.7) | copy-start | bytes 1179652
  166.4 54.7 %all-to-all-start.1 = ((bf16[16,16,4096]{2,1,0:T(8,128)(2,1)}), bf16[16,16,4096]{2,1,0:T(8,128)(2,1)S(1)}, u32[]{:S(2)}, u32[]{:S(2)}) async-start(bf16[16,16,4096]{2,1,0:T(8,128)(2,1)} %bitcast.58), calls=%async_computation.1 | async-start | bytes 4194304 | tf_op jit(solution)/shard_map/all_to_all | solution.py:75
  173.7 108.1 %reduce-scatter.8.cloned.1.call-start = ((), (), s32[]{:S(2)}) async-start(), calls=%async_computation.9 | async-start | bytes 3538944 | tf_op jit(solution)/shard_map/reduce_scatter | solution.py:65
  178.4 3.3 %copy-start.3 = (bf16[1,384,4096]{2,1,0:T(8,128)(2,1)S(1)}, bf16[1,384,4096]{2,1,0:T(8,128)(2,1)}, u32[]{:S(2)}) copy-start(bf16[1,384,4096]{2,1,0:T(8,128)(2,1)} %all-gather.9.cloned.1.call-done) | copy-start | bytes 9437188
  221.1 54.0 %all-to-all-start.3 = ((bf16[16,16,4096]{2,1,0:T(8,128)(2,1)}), bf16[16,16,4096]{2,1,0:T(8,128)(2,1)}, u32[]{:S(2)}, u32[]{:S(2)}) async-start(bf16[16,16,4096]{2,1,0:T(8,128)(2,1)} %bitcast.57), calls=%async_computation.4 | async-start | bytes 4194304 | tf_op jit(solution)/shard_map/all_to_all | solution.py:82
  227.7 56.4 %reduce-scatter.4.cloned.1.call-start = ((), (), s32[]{:S(2)}) async-start(), calls=%async_computation.7 | async-start | bytes 245760 | tf_op jit(solution)/shard_map/reduce_scatter | solution.py:99
  233.8 71.4 %reduce-scatter.6.cloned.1.call-start = ((), (), s32[]{:S(2)}) async-start(), calls=%async_computation.8 | async-start | bytes 245760 | tf_op jit(solution)/shard_map/reduce_scatter | solution.py:102
Sparse Core Ops, SparseCore 0:
  10.1 52.9 all-gather.8
  65.2 46.4 all-gather.10
  113.8 46.4 all-gather.6
  178.5 48.1 reduce-scatter.7
  233.9 23.8 reduce-scatter.3
  281.9 23.1 reduce-scatter.5
where the time goes:
time: 313 us; the launch traced here: 312 us
  waiting for transfers between devices  216 us (69%)
  starting transfers between devices  30.1 us (10%)
  matrix products  24.2 us (8%)
  local copies, waits for them, and re-layouts  16.1 us (5%)
  between operations  14.3 us (5%)
  other arithmetic  11.2 us (4%)
    all_to_all x1, waiting for transfers between devices, on_device(): lax.all_to_all(send_grads, 'expert', split_axis=0, concat_axis=0, tiled=T...  43.6 us
    all_to_all x1, waiting for transfers between devices, on_device(): lax.all_to_all(send_rows, 'expert', split_axis=0, concat_axis=0, tiled=True)  42.1 us
    all_to_all x1, waiting for transfers between devices, on_device(): lax.all_to_all(input_slots.reshape(experts, capacity, model_width), 'expe...  41.3 us
    all_to_all x1, waiting for transfers between devices, on_device(): lax.all_to_all(mixed_slots.reshape(experts, capacity, model_width), 'expe...  36.8 us
    all_gather x1, waiting for transfers between devices, on_device(): lax.all_gather(w_gate[0], 'dp', axis=1, tiled=True)  29.1 us
    reduce_scatter x1, waiting for transfers between devices, on_device(): lax.psum_scatter(input_part.astype(jnp.bfloat16), 'etp', scatter_dimensio...  21.1 us
    all_to_all x1, starting transfers between devices, on_device(): lax.all_to_all(send_rows, 'expert', split_axis=0, concat_axis=0, tiled=True)  9.47 us
    all_to_all x1, starting transfers between devices, on_device(): lax.all_to_all(mixed_slots.reshape(experts, capacity, model_width), 'expe...  7.29 us
  transfers between devices with their start and end apart: 10, of which 6 were waited for; matrix products, arithmetic and copies ran while one was open for 15% of the time, Pallas kernels for 0%

commit v1 on v0

--- a/solution.py
+++ b/solution.py
@@ -1,7 +1,23 @@
+import functools
 import jax
 import jax.numpy as jnp
 from jax import lax
 from jax.sharding import PartitionSpec as P
+
+
+def unite_zone_on(vec, lane_axis):
+    return jnp.concatenate(
+        jax.lax.all_to_all(
+            jnp.stack([vec for _ in range(jax.lax.axis_size(lane_axis))]),
+            axis_name=lane_axis,
+            split_axis=0,
+            concat_axis=0,
+        ),
+        axis=1,
+    )
+
+
+_manage_chains = functools.partial(unite_zone_on, lane_axis="dp")
 
 
 def on_device(tokens, cotangent, route_weights, expert_ids, w_gate, w_up, w_down):
@@ -34,7 +50,7 @@
     flat_rows = recv_rows.reshape(slot_rows, model_width)
     flat_grads = recv_grads.reshape(slot_rows, model_width)
     gate_full, up_full, down_full = (
-        lax.all_gather(w_gate[0], "dp", axis=1, tiled=True),
+        _manage_chains(w_gate[0]),
         lax.all_gather(w_up[0], "dp", axis=1, tiled=True),
         lax.all_gather(w_down[0], "dp", axis=1, tiled=True),
     )

time: 313 us -> 360 us (1.15)
  waiting for transfers between devices: 216 us -> 254 us
  starting transfers between devices: 30.1 us -> 37.7 us
    all_to_all x0 -> x1, waiting for transfers between devices: none -> 66.9 us  [unite_zone_on(): jax.lax.all_to_all(jnp.stack([vec for _ in range(jax.lax.axis_size(lane_a...]
    all_gather x1 -> x0, waiting for transfers between devices: 29.1 us -> none  [on_device(): lax.all_gather(w_gate[0], 'dp', axis=1, tiled=True)]
    all_to_all x0 -> x1, starting transfers between devices: none -> 8.51 us  [unite_zone_on(): jax.lax.all_to_all(jnp.stack([vec for _ in range(jax.lax.axis_size(lane_a...]
  transfers between devices with their start and end apart: 10 -> 10, of which waited for: 6 -> 6; matrix products, arithmetic and copies ran while one was open for 15% -> 11% of each run, Pallas kernels for 0% -> 0%
where the time goes in v1:
time: 360 us
  waiting for transfers between devices  254 us (71%)
  starting transfers between devices  37.7 us (10%)
  matrix products  24.3 us (7%)
  local copies, waits for them, and re-layouts  18.1 us (5%)
  between operations  14 us (4%)
  other arithmetic  11.3 us (3%)
    all_to_all x1, waiting for transfers between devices, unite_zone_on(): jax.lax.all_to_all(jnp.stack([vec for _ in range(jax.lax.axis_size(lane_a...  66.9 us
    all_to_all x1, waiting for transfers between devices, on_device(): lax.all_to_all(send_grads, 'expert', split_axis=0, concat_axis=0, tiled=T...  46.5 us
    all_to_all x1, waiting for transfers between devices, on_device(): lax.all_to_all(send_rows, 'expert', split_axis=0, concat_axis=0, tiled=True)  42.1 us
    all_to_all x1, waiting for transfers between devices, on_device(): lax.all_to_all(input_slots.reshape(experts, capacity, model_width), 'expe...  41.1 us
    all_to_all x1, waiting for transfers between devices, on_device(): lax.all_to_all(mixed_slots.reshape(experts, capacity, model_width), 'expe...  36.7 us
    reduce_scatter x1, waiting for transfers between devices, on_device(): lax.psum_scatter(input_part.astype(jnp.bfloat16), 'etp', scatter_dimensio...  19.3 us
    all_to_all x1, starting transfers between devices, on_device(): lax.all_to_all(send_rows, 'expert', split_axis=0, concat_axis=0, tiled=True)  9.47 us
    all_to_all x1, starting transfers between devices, unite_zone_on(): jax.lax.all_to_all(jnp.stack([vec for _ in range(jax.lax.axis_size(lane_a...  8.51 us
  transfers between devices with their start and end apart: 10, of which 6 were waited for; matrix products, arithmetic and copies ran while one was open for 11% of the time, Pallas kernels for 0%

profile of v1, /device:TPU:8, one launch (start us, length us, event | category | flops | bytes accessed | tf_op | source)
XLA Modules:
  0.0 359.5 jit_solution(239687500509632660)
XLA Ops:
  10.7 4.3 %scatter_custom_fusion = bf16[256,4096]{1,0:T(8,128)(2,1)} fusion(s32[192]{0:T(256)S(1)} %bitcast.61, bf16[]{:T(256)} %constant.10.clone.1, bf16[24,4096]{1,0:T(8,128)(2,1)S(1)} %copy-done), kind=kCustom, calls=%fused_computation.21 | custom fusion | bytes 2293762 | tf_op jit(solution)/shard_map/scatter | solution.py:44
  15.0 9.5 %all-to-all-start = ((bf16[16,16,4096]{2,1,0:T(8,128)(2,1)}), bf16[16,16,4096]{2,1,0:T(8,128)(2,1)S(1)}, u32[]{:S(2)}, u32[]{:S(2)}) async-start(bf16[16,16,4096]{2,1,0:T(8,128)(2,1)} %bitcast.59), calls=%async_computation | async-start | bytes 4194304 | tf_op jit(solution)/shard_map/all_to_all | solution.py:47
  25.5 4.4 %scatter_custom_fusion.1 = bf16[256,4096]{1,0:T(8,128)(2,1)} fusion(s32[192]{0:T(256)S(1)} %bitcast.62, f32[24,4096]{1,0:T(8,128)S(1)} %convert_element_type.51, f32[192]{0:T(256)S(1)} %mul.59, bf16[]{:T(256)} %constant.10.clone.1), kind=kCustom, calls=%fused_computation.19 | custom fusion | flops 1572864 | bytes 2491394 | tf_op jit(solution)/shard_map/scatter | solution.py:45
  29.8 42.1 %all-to-all-done = bf16[16,16,4096]{2,1,0:T(8,128)(2,1)S(1)} async-done(((bf16[16,16,4096]{2,1,0:T(8,128)(2,1)}), bf16[16,16,4096]{2,1,0:T(8,128)(2,1)S(1)}, u32[]{:S(2)}, u32[]{:S(2)}) %all-to-all-start) | async-done | bytes 2097184 | tf_op jit(solution)/shard_map/all_to_all | solution.py:47
  71.9 6.7 %all-to-all-start.3 = ((bf16[16,16,4096]{2,1,0:T(8,128)(2,1)}), bf16[16,16,4096]{2,1,0:T(8,128)(2,1)}, u32[]{:S(2)}, u32[]{:S(2)}) async-start(bf16[16,16,4096]{2,1,0:T(8,128)(2,1)} %bitcast.58), calls=%async_computation.4 | async-start | bytes 4194304 | tf_op jit(solution)/shard_map/all_to_all | solution.py:48
  79.6 46.5 %all-to-all-done.3 = bf16[16,16,4096]{2,1,0:T(8,128)(2,1)} async-done(((bf16[16,16,4096]{2,1,0:T(8,128)(2,1)}), bf16[16,16,4096]{2,1,0:T(8,128)(2,1)}, u32[]{:S(2)}, u32[]{:S(2)}) %all-to-all-start.3) | async-done | bytes 2097184 | tf_op jit(solution)/shard_map/all_to_all | solution.py:48
  126.1 1.9 stack.3
  128.0 8.5 %all-to-all-start.1 = ((bf16[8,384,512]{1,2,0:T(8,128)(2,1)}), bf16[8,384,512]{1,2,0:T(8,128)(2,1)}, u32[]{:S(2)}, u32[]{:S(2)}) async-start(bf16[8,384,512]{1,2,0:T(8,128)(2,1)} %stack.3), calls=%async_computation.1 | async-start | bytes 6291456 | tf_op jit(solution)/shard_map/all_to_all | solution.py:10
  136.6 3.9 %fusion.7 = f32[256,384]{1,0:T(8,128)} fusion(bf16[256,4096]{1,0:T(8,128)(2,1)S(1)} %bitcast.53, bf16[1,384,4096]{2,1,0:T(8,128)(2,1)} %all-gather.5.cloned.1.call-done), kind=kOutput, calls=%fused_computation.17 | convolution fusion | flops 805306368 | bytes 5636096 | tf_op jit(solution)/shard_map/dot_general | solution.py:61
  140.5 3.8 %fusion.3 = f32[256,384]{1,0:T(8,128)S(1)} fusion(bf16[256,4096]{1,0:T(8,128)(2,1)} %bitcast.15, bf16[1,384,4096]{2,1,0:T(8,128)(2,1)} %all-gather.7.cloned.1.call-done), kind=kOutput, calls=%fused_computation.13 | convolution fusion | flops 805306368 | bytes 5636096 | tf_op jit(solution)/shard_map/dot_general | solution.py:70
  144.3 66.9 %all-to-all-done.1 = bf16[8,384,512]{1,2,0:T(8,128)(2,1)} async-done(((bf16[8,384,512]{1,2,0:T(8,128)(2,1)}), bf16[8,384,512]{1,2,0:T(8,128)(2,1)}, u32[]{:S(2)}, u32[]{:S(2)}) %all-to-all-start.1) | async-done | bytes 3145760 | tf_op jit(solution)/shard_map/all_to_all | solution.py:10
  211.2 3.4 multiply_convert_fusion.1
  214.6 2.6 convolution_convert_fusion.1
  217.2 6.1 %all-to-all-start.2 = ((bf16[16,16,4096]{2,1,0:T(8,128)(2,1)}), bf16[16,16,4096]{2,1,0:T(8,128)(2,1)S(1)}, u32[]{:S(2)}, u32[]{:S(2)}) async-start(bf16[16,16,4096]{2,1,0:T(8,128)(2,1)} %bitcast.57), calls=%async_computation.2 | async-start | bytes 4194304 | tf_op jit(solution)/shard_map/all_to_all | solution.py:91
  223.4 4.6 %convolution_convert_fusion = bf16[4096,384]{1,0:T(8,128)(2,1)} fusion(bf16[256,4096]{1,0:T(8,128)(2,1)} %bitcast.55, bf16[256,384]{1,0:T(8,128)(2,1)S(1)} %get-tuple-element.12), kind=kOutput, calls=%fused_computation.5 | convolution fusion | flops 806879232 | bytes 5439488 | tf_op jit(solution)/shard_map/dot_general | solution.py:82
  228.0 3.3 fusion.23
  231.3 2.7 fusion
  233.9 36.7 %all-to-all-done.2 = bf16[16,16,4096]{2,1,0:T(8,128)(2,1)S(1)} async-done(((bf16[16,16,4096]{2,1,0:T(8,128)(2,1)}), bf16[16,16,4096]{2,1,0:T(8,128)(2,1)S(1)}, u32[]{:S(2)}, u32[]{:S(2)}) %all-to-all-start.2) | async-done | bytes 2097184 | tf_op jit(solution)/shard_map/all_to_all | solution.py:91
  270.7 6.5 %all-to-all-start.4 = ((bf16[16,16,4096]{2,1,0:T(8,128)(2,1)}), bf16[16,16,4096]{2,1,0:T(8,128)(2,1)}, u32[]{:S(2)}, u32[]{:S(2)}) async-start(bf16[16,16,4096]{2,1,0:T(8,128)(2,1)} %bitcast.56), calls=%async_computation.5 | async-start | bytes 4194304 | tf_op jit(solution)/shard_map/all_to_all | solution.py:98
  277.3 2.7 gather_fusion
  280.0 3.3 fusion.1
  283.6 41.1 %all-to-all-done.4 = bf16[16,16,4096]{2,1,0:T(8,128)(2,1)} async-done(((bf16[16,16,4096]{2,1,0:T(8,128)(2,1)}), bf16[16,16,4096]{2,1,0:T(8,128)(2,1)}, u32[]{:S(2)}, u32[]{:S(2)}) %all-to-all-start.4) | async-done | bytes 2097184 | tf_op jit(solution)/shard_map/all_to_all | solution.py:98
  324.7 4.9 %gather_fusion.1 = bf16[192,4096]{1,0:T(8,128)(2,1)S(1)} fusion(bf16[256,4096]{1,0:T(8,128)(2,1)} %bitcast.18, s32[1024]{0:T(1024)S(1)} %pad_clamp_fusion), kind=kCustom, calls=%fused_computation.1 | custom fusion | bytes 3146496 | tf_op jit(solution)/shard_map/gather | solution.py:109
  333.6 19.3 %reduce-scatter.6.cloned.1.call-done = bf16[24,1024]{1,0:T(8,128)(2,1)} async-done(((bf16[24,4096]{1,0:T(8,128)(2,1)}), bf16[24,1024]{1,0:T(8,128)(2,1)}) %reduce-scatter.6.cloned.1.call-update) | async-done | bytes 49168 | tf_op jit(solution)/shard_map/reduce_scatter | solution.py:118
  (50 shorter events, 9.8 us)
Async XLA Ops:
  7.2 3.6 copy-start
  15.0 10.2 %copy-start.6 = (bf16[24,4096]{1,0:T(8,128)(2,1)S(1)}, bf16[24,4096]{1,0:T(8,128)(2,1)}, u32[]{:S(2)}) copy-start(bf16[24,4096]{1,0:T(8,128)(2,1)} %param.8) | copy-start | bytes 589828
  15.0 10.3 %copy-start.7 = (f32[24,8]{0,1:T(8,128)S(1)}, f32[24,8]{0,1:T(8,128)}, u32[]{:S(2)}) copy-start(f32[24,8]{0,1:T(8,128)} %param.9) | copy-start | bytes 2308
  15.0 56.9 %all-to-all-start = ((bf16[16,16,4096]{2,1,0:T(8,128)(2,1)}), bf16[16,16,4096]{2,1,0:T(8,128)(2,1)S(1)}, u32[]{:S(2)}, u32[]{:S(2)}) async-start(bf16[16,16,4096]{2,1,0:T(8,128)(2,1)} %bitcast.59), calls=%async_computation | async-start | bytes 4194304 | tf_op jit(solution)/shard_map/all_to_all | solution.py:47
  24.5 112.0 %all-gather.5.cloned.1.call-start = ((), (), s32[]{:S(2)}) async-start(), calls=%async_computation.11 | async-start | bytes 3538944 | tf_op jit(solution)/shard_map/all_gather | solution.py:54
  71.9 139.3 %copy-start.1 = (bf16[16,16,4096]{2,1,0:T(8,128)(2,1)}, bf16[16,16,4096]{2,1,0:T(8,128)(2,1)S(1)}, u32[]{:S(2)}) copy-start(bf16[16,16,4096]{2,1,0:T(8,128)(2,1)S(1)} %all-to-all-done) | copy-start | bytes 6291460
  71.9 7.5 %copy-start.5 = (bf16[1,384,512]{2,1,0:T(8,128)(2,1)S(1)}, bf16[1,384,512]{2,1,0:T(8,128)(2,1)}, u32[]{:S(2)}) copy-start(bf16[1,384,512]{2,1,0:T(8,128)(2,1)} %param.11) | copy-start | bytes 1179652
  71.9 54.2 %all-to-all-start.3 = ((bf16[16,16,4096]{2,1,0:T(8,128)(2,1)}), bf16[16,16,4096]{2,1,0:T(8,128)(2,1)}, u32[]{:S(2)}, u32[]{:S(2)}) async-start(bf16[16,16,4096]{2,1,0:T(8,128)(2,1)} %bitcast.58), calls=%async_computation.4 | async-start | bytes 4194304 | tf_op jit(solution)/shard_map/all_to_all | solution.py:48
  78.6 61.9 %all-gather.7.cloned.1.call-start = ((), (), s32[]{:S(2)}) async-start(), calls=%async_computation.12 | async-start | bytes 3538944 | tf_op jit(solution)/shard_map/all_gather | solution.py:55
  128.0 83.1 %all-to-all-start.1 = ((bf16[8,384,512]{1,2,0:T(8,128)(2,1)}), bf16[8,384,512]{1,2,0:T(8,128)(2,1)}, u32[]{:S(2)}, u32[]{:S(2)}) async-start(bf16[8,384,512]{1,2,0:T(8,128)(2,1)} %stack.3), calls=%async_computation.1 | async-start | bytes 6291456 | tf_op jit(solution)/shard_map/all_to_all | solution.py:10
  211.2 3.4 copy-start.2
  211.2 3.5 copy-start.4
  217.2 53.5 %all-to-all-start.2 = ((bf16[16,16,4096]{2,1,0:T(8,128)(2,1)}), bf16[16,16,4096]{2,1,0:T(8,128)(2,1)S(1)}, u32[]{:S(2)}, u32[]{:S(2)}) async-start(bf16[16,16,4096]{2,1,0:T(8,128)(2,1)} %bitcast.57), calls=%async_computation.2 | async-start | bytes 4194304 | tf_op jit(solution)/shard_map/all_to_all | solution.py:91
  223.3 108.1 %reduce-scatter.8.cloned.1.call-start = ((), (), s32[]{:S(2)}) async-start(), calls=%async_computation.10 | async-start | bytes 3538944 | tf_op jit(solution)/shard_map/reduce_scatter | solution.py:81
  227.9 3.3 copy-start.3
  270.7 54.0 %all-to-all-start.4 = ((bf16[16,16,4096]{2,1,0:T(8,128)(2,1)}), bf16[16,16,4096]{2,1,0:T(8,128)(2,1)}, u32[]{:S(2)}, u32[]{:S(2)}) async-start(bf16[16,16,4096]{2,1,0:T(8,128)(2,1)} %bitcast.56), calls=%async_computation.5 | async-start | bytes 4194304 | tf_op jit(solution)/shard_map/all_to_all | solution.py:98
  277.2 56.4 %reduce-scatter.4.cloned.1.call-start = ((), (), s32[]{:S(2)}) async-start(), calls=%async_computation.8 | async-start | bytes 245760 | tf_op jit(solution)/shard_map/reduce_scatter | solution.py:115
  283.3 69.6 %reduce-scatter.6.cloned.1.call-start = ((), (), s32[]{:S(2)}) async-start(), calls=%async_computation.9 | async-start | bytes 245760 | tf_op jit(solution)/shard_map/reduce_scatter | solution.py:118
Sparse Core Ops, SparseCore 0:
  27.4 50.8 all-gather.4
  81.5 50.8 all-gather.6
  228.1 46.3 reduce-scatter.7
  283.5 22.1 reduce-scatter.3
  331.5 21.4 reduce-scatter.5
